TPU v7x, 256 devices: a whole 4x4x8 slice. The times are simulated.
256 devices in a mesh: row: 16 (over z_lo, y), col: 8 (over x, core), layer: 2 (over z_hi).
Axes of the slice: x: 4, y: 4, z: 8 (z_hi: 2, z_lo: 4; z = z_hi * 4 + z_lo), core: 2. Of those that a mesh axis runs over, the one named last changes fastest.
Arguments:
- density: float32 [2, 8192, 2048], P('layer', 'row', 'col'), may hold values from -6 to 6
- dens_mask: int32 [2, 128, 32], P('layer', 'row', 'col'), may hold values from 0 to 1, as said below
- hamiltonian: float32 [2, 2048, 16384], P('layer', 'row', 'col'), may hold values from -0.375 to 0.375
- ham_mask: int32 [2, 32, 256], P('layer', None, 'col'), may hold values from 0 to 1, as said below
- filter_mask: int32 [128, 256], P('row', 'col'), may hold values from 0 to 1, as said below
Outputs:
- product: float32 [8192, 16384], P('row', ('col', 'layer'))
Inputs may be any that keep to these rules, and one draw needn't show every extreme that they name: `dens_mask`: 1 where a density block is nonzero, else 0. `ham_mask`: 1 where a Hamiltonian block is nonzero, else 0. `filter_mask`: 1 where a result block is kept, else 0.
All inputs are finite; a program needn't handle non-finite values.
Results may differ from a plain program's by a relative error of at most 0.0001.
Values sent between devices are 32-bit elements; how exact they have to be, the bound alone decides.
No kernel may reach another device: no remote copies, remote signals or barrier semaphores. Data moves between devices by JAX's collectives and lax.ppermute only.
A program may use at most 128 MiB of HBM per device.

v0:
```python
import jax
import jax.numpy as jnp
from jax import lax
from jax.sharding import PartitionSpec as P

BLOCK = 64


def expand(block_mask):
    widened = jnp.repeat(block_mask.astype(jnp.float32), BLOCK, axis=-2)
    return jnp.repeat(widened, BLOCK, axis=-1)


def shards(density, dens_mask, hamiltonian, ham_mask, filter_mask):
    dens_vals = density * expand(dens_mask)
    ham_count = hamiltonian.shape[1]
    row_ids = lax.axis_index("row") * ham_count + jnp.arange(ham_count, dtype=jnp.int32)
    block_ids = row_ids // BLOCK
    one_hot = (
        block_ids[:, None] == jnp.arange(ham_mask.shape[1], dtype=jnp.int32)[None, :]
    ).astype(jnp.float32)
    picked = jnp.dot(
        one_hot,
        ham_mask[0].astype(jnp.float32),
        precision=lax.Precision.HIGHEST,
        preferred_element_type=jnp.float32,
    )
    ham_vals = hamiltonian * jnp.repeat(picked, BLOCK, axis=1)[None]
    kept = expand(filter_mask)
    ham_group = lax.all_gather(ham_vals, "row", axis=1, tiled=True)
    ham_part = ham_group[0]
    partial_value = jnp.dot(
        lax.all_gather(dens_vals, "col", axis=2, tiled=True)[0],
        ham_part,
        precision=lax.Precision.HIGHEST,
        preferred_element_type=jnp.float32,
    )
    return lax.psum_scatter(partial_value * kept, "layer", scatter_dimension=1, tiled=True)


def solution(mesh):
    return jax.shard_map(
        shards,
        mesh=mesh,
        in_specs=(
            P("layer", "row", "col"),
            P("layer", "row", "col"),
            P("layer", "row", "col"),
            P("layer", None, "col"),
            P("row", "col"),
        ),
        out_specs=P("row", ("col", "layer")),
        check_vma=False,
    )
```

profile of v0, /device:TPU:1, one launch (start us, length us, event | category | flops | bytes accessed | tf_op | source)
XLA Modules:
  0.0 426.2 jit_solution(16033029685912236478)
XLA Ops:
  6.5 0.0 copy-start.1
  6.5 0.0 copy-start
  6.5 0.0 all-gather.3.cloned.1.call-start
  6.5 1.3 copy.8
  7.8 0.7 convert_bitcast_fusion
  8.5 0.1 broadcast_in_dim.21
  8.6 0.1 broadcast_in_dim.22
  8.7 0.9 bitcast_multiply_fusion.1
  9.5 0.0 all-gather.3.cloned.1.call-update
  9.6 0.0 all-gather.5.cloned.1.call-start
  9.6 1.6 copy.9
  11.2 0.0 copy-done.1
  11.2 0.2 fusion.8
  11.4 1.1 bitcast_multiply_fusion
  12.5 0.0 all-gather.5.cloned.1.call-update
  12.5 0.0 reduce-scatter.2.cloned.1.call-start
  12.6 0.0 copy-done
  12.6 0.1 copy.10
  12.7 0.1 broadcast_in_dim.26
  12.8 0.1 reshape.35
  12.9 2.5 broadcast_in_dim.27
  15.4 5.5 %copy.11 = f32[512,2048]{1,0:T(8,128)} copy(f32[512,2048]{0,1:T(8,128)} %bitcast.24) | data formatting | bytes 8388608 | tf_op jit(solution)/shard_map/reshape | solution.py:11
  20.8 27.6 %all-gather.3.cloned.1.call-done = f32[1,512,2048]{1,2,0:T(8,128)} async-done(((f32[1,512,256]{1,2,0:T(8,128)}), f32[1,512,2048]{1,2,0:T(8,128)}) %all-gather.3.cloned.1.call-update) | async-done | bytes 4194320 | tf_op jit(solution)/shard_map/all_gather | solution.py:33
  48.5 194.2 %all-gather.5.cloned.1.call-done = f32[1,2048,2048]{1,2,0:T(8,128)} async-done(((f32[1,128,2048]{1,2,0:T(8,128)}), f32[1,2048,2048]{1,2,0:T(8,128)}) %all-gather.5.cloned.1.call-update) | async-done | bytes 16777232 | tf_op jit(solution)/shard_map/all_gather | solution.py:30
  242.7 57.7 %fusion.3 = f32[512,2048]{1,0:T(8,128)} fusion(f32[512,2048]{1,0:T(8,128)} %copy.11, f32[1,2048,2048]{1,2,0:T(8,128)} %all-gather.5.cloned.1.call-done, f32[1,512,2048]{1,2,0:T(8,128)} %all-gather.3.cloned.1.call-done), kind=kOutput, calls=%fused_computation.3 | convolution fusion | flops 25770852352 | bytes 29360128 | tf_op jit(solution)/shard_map/dot_general | solution.py:32
  300.3 0.0 reduce-scatter.2.cloned.1.call-update
  300.3 119.4 %reduce-scatter.2.cloned.1.call-done = f32[512,1024]{1,0:T(8,128)} async-done(((f32[512,2048]{1,0:T(8,128)}), f32[512,1024]{1,0:T(8,128)}) %reduce-scatter.2.cloned.1.call-update) | async-done | bytes 2097168 | tf_op jit(solution)/shard_map/reduce_scatter | solution.py:38
  (2 shorter events, 0.0 us)
Async XLA Ops:
  6.5 4.7 %copy-start.1 = (s32[1,32,32]{2,1,0:T(8,128)S(1)}, s32[1,32,32]{2,1,0:T(8,128)}, u32[]{:S(2)}) copy-start(s32[1,32,32]{2,1,0:T(8,128)} %param.8) | copy-start | bytes 12292
  6.5 6.1 %copy-start = (s32[8,32]{1,0:T(8,128)S(1)}, s32[8,32]{1,0:T(8,128)}, u32[]{:S(2)}) copy-start(s32[8,32]{1,0:T(8,128)} %param.9) | copy-start | bytes 3076
  6.5 41.9 %all-gather.3.cloned.1.call-start = ((), (), s32[]{:S(2)}) async-start(), calls=%async_computation.1 | async-start | bytes 4718592 | tf_op jit(solution)/shard_map/all_gather | solution.py:33
  9.6 233.1 %all-gather.5.cloned.1.call-start = ((), (), s32[]{:S(2)}) async-start(), calls=%async_computation.2 | async-start | bytes 17825792 | tf_op jit(solution)/shard_map/all_gather | solution.py:30
  12.5 407.2 %reduce-scatter.2.cloned.1.call-start = ((), (), s32[]{:S(2)}) async-start(), calls=%async_computation.3 | async-start | bytes 6291456 | tf_op jit(solution)/shard_map/reduce_scatter | solution.py:38
Sparse Core Ops, SparseCore 0:
  9.7 38.7 all-gather.2
  50.2 192.4 all-gather.4
  300.5 119.2 reduce-scatter.1
where the time goes:
time: 426 us
  waiting for transfers between devices  341 us (80%)
  matrix products  57.9 us (14%)
  between operations  13.2 us (3%)
  local copies, waits for them, and re-layouts  11.2 us (3%)
    all_gather x1, waiting for transfers between devices, shards(): ham_group = lax.all_gather(ham_vals, 'row', axis=1, tiled=True)  194 us
    reduce_scatter x1, waiting for transfers between devices, shards(): lax.psum_scatter(partial_value * kept, 'layer', scatter_dimension=1, tile...  119 us
    dot_general x1, matrix products, shards(): jnp.dot(lax.all_gather(dens_vals, 'col', axis=2, tiled=True)[0], ham_part...  57.7 us
    all_gather x1, waiting for transfers between devices, shards(): lax.all_gather(dens_vals, 'col', axis=2, tiled=True)[0]  27.6 us
  transfers between devices with their start and end apart: 3, of which 3 were waited for; matrix products, arithmetic and copies ran while one was open for 3% of the time, Pallas kernels for 0%

commit v1 on v0

--- a/solution.py
+++ b/solution.py
@@ -4,6 +4,11 @@
 from jax.sharding import PartitionSpec as P
 
 BLOCK = 64
+
+
+def all_by_exchange(shard, mesh_axis, dim):
+    sent = jnp.stack([shard] * lax.axis_size(mesh_axis))
+    return jnp.concatenate(lax.all_to_all(sent, mesh_axis, 0, 0), axis=dim)
 
 
 def expand(block_mask):
@@ -30,7 +35,7 @@
     ham_group = lax.all_gather(ham_vals, "row", axis=1, tiled=True)
     ham_part = ham_group[0]
     partial_value = jnp.dot(
-        lax.all_gather(dens_vals, "col", axis=2, tiled=True)[0],
+        all_by_exchange(dens_vals, "col", 2)[0],
         ham_part,
         precision=lax.Precision.HIGHEST,
         preferred_element_type=jnp.float32,

time: 426 us -> 391 us (0.918)
  waiting for transfers between devices: 341 us -> 297 us
  starting transfers between devices: 0.09 us -> 7.78 us
    all_gather x1, waiting for transfers between devices: 194 us -> 137 us  [shards(): ham_group = lax.all_gather(ham_vals, 'row', axis=1, tiled=True)]
    all_to_all x0 -> x1, waiting for transfers between devices: none -> 40.6 us  [all_by_exchange(): return jnp.concatenate(lax.all_to_all(sent, mesh_axis, 0, 0), axis=dim)]
    all_gather x1 -> x0, waiting for transfers between devices: 27.6 us -> none  [shards(): lax.all_gather(dens_vals, 'col', axis=2, tiled=True)[0]]
    all_to_all x0 -> x1, starting transfers between devices: none -> 7.77 us  [all_by_exchange(): return jnp.concatenate(lax.all_to_all(sent, mesh_axis, 0, 0), axis=dim)]
where the time goes in v1:
time: 391 us
  waiting for transfers between devices  297 us (76%)
  matrix products  58.6 us (15%)
  between operations  13.5 us (3%)
  local copies, waits for them, and re-layouts  12.7 us (3%)
  starting transfers between devices  7.78 us (2%)
    all_gather x1, waiting for transfers between devices, shards(): ham_group = lax.all_gather(ham_vals, 'row', axis=1, tiled=True)  137 us
    reduce_scatter x1, waiting for transfers between devices, shards(): lax.psum_scatter(partial_value * kept, 'layer', scatter_dimension=1, tile...  119 us
    dot_general x1, matrix products, shards(): jnp.dot(all_by_exchange(dens_vals, 'col', 2)[0], ham_part, precision=lax....  57.6 us
    all_to_all x1, waiting for transfers between devices, all_by_exchange(): return jnp.concatenate(lax.all_to_all(sent, mesh_axis, 0, 0), axis=dim)  40.6 us
  transfers between devices with their start and end apart: 3, of which 3 were waited for; matrix products, arithmetic and copies ran while one was open for 3% of the time, Pallas kernels for 0%

profile of v1, /device:TPU:1, one launch (start us, length us, event | category | flops | bytes accessed | tf_op | source)
XLA Modules:
  0.0 390.9 jit_solution(1963832733471518998)
XLA Ops:
  6.5 0.0 copy-start
  6.5 0.0 copy-start.2
  6.5 0.0 all-gather.2.cloned.1.call-start
  6.5 1.6 copy.14
  8.2 0.9 fusion.5
  9.1 1.1 bitcast_multiply_fusion
  10.2 0.0 all-gather.2.cloned.1.call-update
  10.2 0.0 copy-done
  10.2 0.2 copy.12
  10.4 0.0 copy-done.2
  10.5 0.1 broadcast_in_dim.21
  10.5 0.1 broadcast_in_dim.22
  10.6 0.1 bitcast_multiply_fusion.1
  10.7 2.5 stack.2
  13.2 0.0 copy-start.1
  13.2 7.8 %all-to-all-start = ((f32[8,1,512,256]{2,3,1,0:T(8,128)}), f32[8,1,512,256]{2,3,1,0:T(8,128)}, u32[]{:S(2)}, u32[]{:S(2)}) async-start(f32[8,1,512,256]{2,3,1,0:T(8,128)} %stack.2), calls=%async_computation | async-start | bytes 8388608 | tf_op jit(solution)/shard_map/all_to_all | solution.py:11
  21.0 0.0 reduce-scatter.2.cloned.1.call-start
  21.0 0.0 copy-done.1
  21.0 0.1 copy.15
  21.1 0.1 broadcast_in_dim.26
  21.2 0.1 reshape.42
  21.3 2.5 broadcast_in_dim.27
  23.7 5.5 %copy.16 = f32[512,2048]{1,0:T(8,128)} copy(f32[512,2048]{0,1:T(8,128)} %bitcast.26) | data formatting | bytes 8388608 | tf_op jit(solution)/shard_map/reshape | solution.py:16
  29.2 40.6 %all-to-all-done = f32[8,1,512,256]{2,3,1,0:T(8,128)} async-done(((f32[8,1,512,256]{2,3,1,0:T(8,128)}), f32[8,1,512,256]{2,3,1,0:T(8,128)}, u32[]{:S(2)}, u32[]{:S(2)}) %all-to-all-start) | async-done | bytes 4194336 | tf_op jit(solution)/shard_map/all_to_all | solution.py:11
  69.8 137.2 %all-gather.2.cloned.1.call-done = f32[1,2048,2048]{1,2,0:T(8,128)} async-done(((f32[1,128,2048]{1,2,0:T(8,128)}), f32[1,2048,2048]{1,2,0:T(8,128)}) %all-gather.2.cloned.1.call-update) | async-done | bytes 16777232 | tf_op jit(solution)/shard_map/all_gather | solution.py:35
  207.0 57.6 %fusion.2 = f32[512,2048]{1,0:T(8,128)} fusion(f32[512,2048]{1,0:T(8,128)} %copy.16, f32[512,2048]{0,1:T(8,128)} %bitcast.5, f32[1,2048,2048]{1,2,0:T(8,128)} %all-gather.2.cloned.1.call-done), kind=kOutput, calls=%fused_computation.2 | convolution fusion | flops 25770852352 | bytes 29360128 | tf_op jit(solution)/shard_map/dot_general | solution.py:37
  264.6 0.0 reduce-scatter.2.cloned.1.call-update
  264.7 119.4 %reduce-scatter.2.cloned.1.call-done = f32[512,1024]{1,0:T(8,128)} async-done(((f32[512,2048]{1,0:T(8,128)}), f32[512,1024]{1,0:T(8,128)}) %reduce-scatter.2.cloned.1.call-update) | async-done | bytes 2097168 | tf_op jit(solution)/shard_map/reduce_scatter | solution.py:43
  (3 shorter events, 0.0 us)
Async XLA Ops:
  6.5 3.7 copy-start
  6.5 3.9 copy-start.2
  6.5 200.5 %all-gather.2.cloned.1.call-start = ((), (), s32[]{:S(2)}) async-start(), calls=%async_computation.2 | async-start | bytes 17825792 | tf_op jit(solution)/shard_map/all_gather | solution.py:35
  13.2 7.8 %copy-start.1 = (s32[8,32]{1,0:T(8,128)S(1)}, s32[8,32]{1,0:T(8,128)}, u32[]{:S(2)}) copy-start(s32[8,32]{1,0:T(8,128)} %param.9) | copy-start | bytes 3076
  13.2 56.6 %all-to-all-start = ((f32[8,1,512,256]{2,3,1,0:T(8,128)}), f32[8,1,512,256]{2,3,1,0:T(8,128)}, u32[]{:S(2)}, u32[]{:S(2)}) async-start(f32[8,1,512,256]{2,3,1,0:T(8,128)} %stack.2), calls=%async_computation | async-start | bytes 8388608 | tf_op jit(solution)/shard_map/all_to_all | solution.py:11
  21.0 363.1 %reduce-scatter.2.cloned.1.call-start = ((), (), s32[]{:S(2)}) async-start(), calls=%async_computation.3 | async-start | bytes 6291456 | tf_op jit(solution)/shard_map/reduce_scatter | solution.py:43
Sparse Core Ops, SparseCore 0:
  10.3 196.6 all-gather.1
  264.8 119.2 reduce-scatter.1
